TPU v7x, 32 devices: a whole 2x2x4 slice. The times are simulated.
32 devices in a mesh: ctx: 8 (over z, core), fsdp: 4 (over y, x).
Axes of the slice: x: 2, y: 2, z: 4, core: 2. Of those that a mesh axis runs over, the one named last changes fastest.
Arguments:
- layer_in: bfloat16 [4, 8, 2, 128, 1024], P(None, 'ctx', None, 'fsdp'), may hold values from -6 to 6
- out_grad: bfloat16 [4, 8, 2, 128, 1024], P(None, 'ctx', None, 'fsdp'), may hold values from -6 to 6
- block_pairs: int32 [4, 8], replicated, may hold values from 0 to 7, each once within a row
- attn_gain: bfloat16 [1024], P('fsdp'), may hold values from 0.099609375 to 1.8984375
- attn_shift: bfloat16 [1024], P('fsdp'), may hold values from -3 to 3
- qkv_weight: bfloat16 [1024, 3072], P('fsdp'), may hold values from -0.25 to 0.25
- query_bias: bfloat16 [1024], P('fsdp'), may hold values from -3 to 3
- value_bias: bfloat16 [1024], P('fsdp'), may hold values from -0.29882812 to 0.29882812
- out_weight: bfloat16 [1024, 1024], P('fsdp'), may hold values from -2 to 2
- out_bias: bfloat16 [1024], P('fsdp'), may hold values from -3 to 3
- mlp_gain: bfloat16 [1024], P('fsdp'), may hold values from 0.099609375 to 1.8984375
- mlp_shift: bfloat16 [1024], P('fsdp'), may hold values from -3 to 3
- fc_weight: bfloat16 [1024, 4096], P('fsdp'), may hold values from -0.1875 to 0.1875
- fc_bias: bfloat16 [4096], P('fsdp'), may hold values from -3 to 3
- proj_weight: bfloat16 [4096, 1024], P('fsdp'), may hold values from -0.09375 to 0.09375
- proj_bias: bfloat16 [1024], P('fsdp'), may hold values from -3 to 3
Outputs:
- layer_out: bfloat16 [4, 8, 2, 128, 1024], P(None, 'ctx', None, 'fsdp')
- in_grad: float32 [4, 8, 2, 128, 1024], P(None, 'ctx', None, 'fsdp')
- attn_gain_grad: float32 [1024], P('fsdp')
- attn_shift_grad: float32 [1024], P('fsdp')
- qkv_weight_grad: float32 [1024, 3072], P('fsdp')
- query_bias_grad: float32 [1024], P('fsdp')
- value_bias_grad: float32 [1024], P('fsdp')
- out_weight_grad: float32 [1024, 1024], P('fsdp')
- out_bias_grad: float32 [1024], P('fsdp')
- mlp_gain_grad: float32 [1024], P('fsdp')
- mlp_shift_grad: float32 [1024], P('fsdp')
- fc_weight_grad: float32 [1024, 4096], P('fsdp')
- fc_bias_grad: float32 [4096], P('fsdp')
- proj_weight_grad: float32 [4096, 1024], P('fsdp')
- proj_bias_grad: float32 [1024], P('fsdp')
Inputs may be any that keep to these rules, and one draw needn't show every extreme that they name: `block_pairs`: each row is a permutation: every device of ctx holds exactly one block pair of every sequence.
All inputs are finite; a program needn't handle non-finite values.
Results may differ from a plain program's by a relative error of at most 0.023.
Values may be sent and summed in bfloat16 or wider, within the bound.
No kernel may reach another device: no remote copies, remote signals or barrier semaphores. Data moves between devices by JAX's collectives and lax.ppermute only.
A program may use at most 320 MiB of HBM per device.

v0:
```python
import jax
import jax.numpy as jnp
from jax import lax
from jax.sharding import PartitionSpec as P

HD = 64
norm_eps = 1e-05
masked_score = -1e30


def for_sending(array):
    return jax.tree.map(lambda a: a.astype(jnp.bfloat16) if a.dtype == jnp.float32 else a, array)


def layer_norm(values, gain, shift):
    average = jnp.mean(values, axis=-1, keepdims=True)
    centred = values - average
    spread = jnp.mean(centred * centred, axis=-1, keepdims=True)
    return centred * lax.rsqrt(spread + norm_eps) * gain + shift


def gelu_tanh(values):
    return jax.nn.gelu(values, approximate=True)


def contract_last(left, right):
    return lax.dot_general(
        left, right, (((1,), (1,)), ((), ())), preferred_element_type=jnp.float32
    )


def contract_first(left, right):
    return lax.dot_general(
        left, right, (((0,), (0,)), ((), ())), preferred_element_type=jnp.float32
    )


def head_scores(query, keys, query_places, key_places):
    scores = contract_last(query, keys)
    return jnp.where(key_places[None, :] <= query_places[:, None], scores, masked_score)


def score_grads(query, keys, values, grad_out, summary, row_sum, query_places, key_places):
    scores = head_scores(query, keys, query_places, key_places)
    probs = jnp.exp(scores - summary[:, None])
    grad_probs = contract_last(grad_out, values)
    row_sum = jnp.sum(probs * grad_probs, axis=1)
    grad_scores = (probs * (grad_probs - row_sum[:, None])).astype(jnp.bfloat16)
    return (probs.astype(jnp.bfloat16), grad_scores, row_sum)


def attend_forward(items):
    query, keys, values, query_places, key_places = items
    outputs = []
    summaries = []
    for head_index in range(query.shape[1] // HD):
        columns = slice(head_index * HD, (head_index + 1) * HD)
        scores = head_scores(query[:, columns], keys[:, columns], query_places, key_places)
        row_peak = jnp.max(scores, axis=1, keepdims=True)
        raised = jnp.exp(scores - row_peak)
        row_total = jnp.sum(raised, axis=1, keepdims=True)
        weights = (raised / row_total).astype(jnp.bfloat16)
        outputs.append(
            jnp.dot(weights, values[:, columns], preferred_element_type=jnp.float32).astype(
                jnp.bfloat16
            )
        )
        summaries.append(row_peak[:, 0] + jnp.log(row_total[:, 0]))
    return (jnp.concatenate(outputs, axis=1), jnp.stack(summaries, axis=1))


def attend_backward(items):
    query, keys, values, grad_out, summary, query_places, key_places = items
    query_parts, key_parts, value_parts = ([], [], [])
    for head_index in range(query.shape[1] // HD):
        columns = slice(head_index * HD, (head_index + 1) * HD)
        probs_low, grad_scores, row_sum = score_grads(
            query[:, columns],
            keys[:, columns],
            values[:, columns],
            grad_out[:, columns],
            summary[:, head_index],
            None,
            query_places,
            key_places,
        )
        query_parts.append(
            jnp.dot(grad_scores, keys[:, columns], preferred_element_type=jnp.float32).astype(
                jnp.bfloat16
            )
        )
        key_parts.append(contract_first(grad_scores, query[:, columns]))
        value_parts.append(contract_first(probs_low, grad_out[:, columns]))
    return (
        jnp.concatenate(query_parts, axis=1),
        jnp.concatenate(key_parts, axis=1),
        jnp.concatenate(value_parts, axis=1),
    )


CTX = ("zc", "core")


def gather_weight(shard):
    half = shard.shape[0] // 2
    piece = lax.dynamic_slice_in_dim(shard, lax.axis_index("core") * half, half, 0)
    fsdp_size = lax.axis_size("fsdp")
    pieces = lax.all_to_all(
        jnp.broadcast_to(piece[None], (fsdp_size,) + piece.shape),
        "fsdp",
        split_axis=0,
        concat_axis=0,
        tiled=True,
    )
    whole = lax.all_gather(pieces, "core", axis=1, tiled=True)
    return whole.reshape(-1, shard.shape[1])


def core_major(rows, fsdp_size):
    count, width = rows.shape
    return (
        rows.reshape(count, fsdp_size, 2, width // (2 * fsdp_size))
        .transpose(0, 2, 1, 3)
        .reshape(count, width)
    )


def reduce_weight_grad(grad):
    grad = lax.psum_scatter(grad.astype(jnp.bfloat16), "core", scatter_dimension=0, tiled=True)
    fsdp_size = lax.axis_size("fsdp")
    blocks = lax.all_to_all(
        grad.reshape((fsdp_size, -1) + grad.shape[1:]),
        "fsdp",
        split_axis=0,
        concat_axis=0,
        tiled=True,
    )
    grad = jnp.sum(blocks.astype(jnp.float32), axis=0).astype(jnp.bfloat16)
    grad = lax.psum_scatter(grad, "zc", scatter_dimension=0, tiled=True)
    grad = lax.all_gather(grad, "zc", axis=0, tiled=True)
    grad = lax.all_gather(grad, "core", axis=0, tiled=True)
    return grad.astype(jnp.float32)


def shards(
    layer_in,
    out_grad,
    block_pairs,
    attn_gain,
    attn_shift,
    qkv_weight,
    query_bias,
    value_bias,
    out_weight,
    out_bias,
    mlp_gain,
    mlp_shift,
    fc_weight,
    fc_bias,
    proj_weight,
    proj_bias,
):
    fsdp_size = lax.axis_size("fsdp")
    ctx_size = lax.axis_size("zc") * lax.axis_size("core")
    seq_count = layer_in.shape[0]
    half_rows = layer_in.shape[3]
    model_width = layer_in.shape[4]
    block_len = half_rows * fsdp_size
    pair_len = 2 * block_len
    group_width = model_width // fsdp_size
    gathered = (
        gather_weight(qkv_weight),
        gather_weight(out_weight),
        gather_weight(fc_weight),
        gather_weight(proj_weight),
    )
    qkv_full, out_full, fc_full, proj_full = (gathered[0], gathered[1], gathered[2], gathered[3])
    vector_shards = (
        attn_gain,
        attn_shift,
        query_bias,
        value_bias,
        out_bias,
        mlp_gain,
        mlp_shift,
        fc_bias,
        proj_bias,
    )
    vector_pieces = lax.all_gather(jnp.concatenate(vector_shards), "fsdp", axis=0, tiled=False)
    vectors = []
    start = 0
    for shard in vector_shards:
        vectors.append(
            vector_pieces[:, start : start + shard.shape[0]].reshape(-1).astype(jnp.float32)
        )
        start += shard.shape[0]
    (
        gain_attn,
        shift_attn,
        bias_query,
        bias_value,
        bias_out,
        gain_mlp,
        shift_mlp,
        bias_fc,
        bias_proj,
    ) = vectors
    halves = jnp.stack([block_pairs, 2 * ctx_size - 1 - block_pairs], axis=2)
    key_places = (halves[..., None] * block_len + jnp.arange(block_len, dtype=jnp.int32)).reshape(
        seq_count, ctx_size, pair_len
    )
    query_places = lax.dynamic_slice_in_dim(key_places, lax.axis_index(CTX), 1, 1).reshape(
        seq_count, pair_len
    )
    key_places = key_places.reshape(seq_count, ctx_size * pair_len)
    inputs = layer_in.reshape(-1, model_width).astype(jnp.float32)
    normed, attn_norm_back = jax.vjp(layer_norm, inputs, gain_attn, shift_attn)
    normed_low = normed.astype(jnp.bfloat16)
    mixed = jnp.dot(normed_low, qkv_full, preferred_element_type=jnp.float32)
    query = ((mixed[:, :model_width] + bias_query) * 0.125).astype(jnp.bfloat16)
    keys = mixed[:, model_width : 2 * model_width].astype(jnp.bfloat16)
    values = (mixed[:, 2 * model_width :] + bias_value).astype(jnp.bfloat16)

    def to_groups(array):
        return array.reshape(seq_count, 2, half_rows, fsdp_size, group_width)

    def to_pairs(array):
        return array.reshape(seq_count, 2, block_len, 1, group_width)

    qkv_heads = lax.all_to_all(
        jnp.concatenate([to_groups(query), to_groups(keys), to_groups(values)], axis=4),
        "fsdp",
        split_axis=3,
        concat_axis=2,
        tiled=True,
    ).reshape(seq_count, pair_len, 3 * group_width)
    query_heads = qkv_heads[..., :group_width]
    own_kv = qkv_heads[..., group_width:]
    kv_all = lax.all_gather(
        own_kv.reshape(seq_count, 1, pair_len, 2 * group_width), CTX, axis=1, tiled=True
    )
    key_all = kv_all[..., :group_width]
    value_all = kv_all[..., group_width:]
    key_all = key_all.reshape(seq_count, -1, group_width)
    value_all = value_all.reshape(seq_count, -1, group_width)
    attended, summary = lax.map(
        attend_forward, (query_heads, key_all, value_all, query_places, key_places)
    )
    attended_rows = lax.all_to_all(
        for_sending(to_pairs(attended)), "fsdp", split_axis=2, concat_axis=3, tiled=True
    ).reshape(-1, model_width)
    branch = jnp.dot(attended_rows, out_full, preferred_element_type=jnp.float32) + bias_out
    middle = inputs + branch
    normed_mlp, mlp_norm_back = jax.vjp(layer_norm, middle, gain_mlp, shift_mlp)
    mlp_low = normed_mlp.astype(jnp.bfloat16)
    hidden = jnp.dot(mlp_low, fc_full, preferred_element_type=jnp.float32) + bias_fc
    activated, gelu_back = jax.vjp(gelu_tanh, hidden)
    activated_low = activated.astype(jnp.bfloat16)
    result = (
        middle + jnp.dot(activated_low, proj_full, preferred_element_type=jnp.float32) + bias_proj
    )
    layer_out = result.astype(jnp.bfloat16).reshape(layer_in.shape)
    grad_rows = out_grad.reshape(-1, model_width)
    grad_result = grad_rows.astype(jnp.float32)
    proj_grad = contract_first(core_major(activated_low, fsdp_size), grad_rows)
    proj_bias_grad = jnp.sum(grad_result, axis=0)
    grad_activated = contract_last(grad_rows, proj_full)
    grad_hidden = gelu_back(grad_activated)[0].astype(jnp.bfloat16)
    fc_grad = contract_first(core_major(mlp_low, fsdp_size), grad_hidden)
    fc_bias_grad = jnp.sum(grad_hidden.astype(jnp.float32), axis=0)
    grad_middle, mlp_gain_grad, mlp_shift_grad = mlp_norm_back(contract_last(grad_hidden, fc_full))
    grad_middle = grad_middle + grad_result
    grad_branch = grad_middle.astype(jnp.bfloat16)
    out_weight_term = contract_first(core_major(attended_rows, fsdp_size), grad_branch)
    out_bias_grad = jnp.sum(grad_branch.astype(jnp.float32), axis=0)
    grad_attended = contract_last(grad_branch, out_full).astype(jnp.bfloat16)
    grad_heads = lax.all_to_all(
        to_groups(grad_attended), "fsdp", split_axis=3, concat_axis=2, tiled=True
    ).reshape(seq_count, pair_len, group_width)
    grad_query, grad_keys, grad_values = lax.map(
        attend_backward,
        (query_heads, key_all, value_all, grad_heads, summary, query_places, key_places),
    )
    kv_grads = jnp.concatenate([grad_keys, grad_values], axis=2).astype(jnp.bfloat16)
    kv_grads = kv_grads.reshape(seq_count, ctx_size, pair_len, 2 * group_width).transpose(
        1, 0, 2, 3
    )
    kv_part = lax.psum_scatter(
        kv_grads.reshape(ctx_size * seq_count * pair_len, 2 * group_width),
        CTX,
        scatter_dimension=0,
        tiled=True,
    ).reshape(seq_count, pair_len, 2 * group_width)
    key_part = kv_part[..., :group_width].astype(jnp.float32)
    value_part = kv_part[..., group_width:].astype(jnp.float32)
    key_grad_low = key_part.astype(jnp.bfloat16)
    value_grad_low = value_part.astype(jnp.bfloat16)
    query_back, key_back, value_back = (
        lax.all_to_all(
            for_sending(to_pairs(grad_query)), "fsdp", split_axis=2, concat_axis=3, tiled=True
        ),
        lax.all_to_all(
            for_sending(to_pairs(key_grad_low)), "fsdp", split_axis=2, concat_axis=3, tiled=True
        ),
        lax.all_to_all(
            for_sending(to_pairs(value_grad_low)), "fsdp", split_axis=2, concat_axis=3, tiled=True
        ),
    )
    grad_mixed = jnp.concatenate(
        [
            query_back.reshape(-1, model_width) * 0.125,
            key_back.reshape(-1, model_width),
            value_back.reshape(-1, model_width),
        ],
        axis=1,
    )
    qkv_grad = contract_first(core_major(normed_low, fsdp_size), grad_mixed)
    mixed_float = grad_mixed.astype(jnp.float32)
    query_bias_grad = jnp.sum(mixed_float[:, :model_width], axis=0)
    value_bias_grad = jnp.sum(mixed_float[:, 2 * model_width :], axis=0)
    grad_inputs, attn_gain_grad, attn_shift_grad = attn_norm_back(
        contract_last(grad_mixed, qkv_full)
    )
    in_grad = (grad_inputs + grad_middle).reshape(layer_in.shape)
    weight_totals = tuple(
        (reduce_weight_grad(grad) for grad in (qkv_grad, out_weight_term, fc_grad, proj_grad))
    )
    vector_grads = (
        attn_gain_grad,
        attn_shift_grad,
        query_bias_grad,
        value_bias_grad,
        out_bias_grad,
        mlp_gain_grad,
        mlp_shift_grad,
        fc_bias_grad,
        proj_bias_grad,
    )
    packed = jnp.concatenate([grad.reshape(fsdp_size, -1) for grad in vector_grads], axis=1)
    packed = lax.psum(packed.astype(jnp.float32), CTX + ("fsdp",))
    packed = lax.dynamic_index_in_dim(packed, lax.axis_index("fsdp"), 0, keepdims=False)
    vector_totals = []
    offset = 0
    for grad in vector_grads:
        width = grad.shape[0] // fsdp_size
        vector_totals.append(packed[offset : offset + width])
        offset += width
    totals = weight_totals + tuple(vector_totals)
    return (
        layer_out,
        in_grad,
        totals[4],
        totals[5],
        totals[0],
        totals[6],
        totals[7],
        totals[1],
        totals[8],
        totals[9],
        totals[10],
        totals[2],
        totals[11],
        totals[3],
        totals[12],
    )


def solution(mesh):
    ctx_count, fsdp_count = mesh.devices.shape
    mesh = jax.sharding.Mesh(
        mesh.devices.reshape(ctx_count // 2, 2, fsdp_count), ("zc", "core", "fsdp")
    )
    placed = (
        P(None, CTX, None, "fsdp", None),
        P(None, CTX, None, "fsdp", None),
        P(),
        P("fsdp"),
        P("fsdp"),
        P("fsdp", None),
        P("fsdp"),
        P("fsdp"),
        P("fsdp", None),
        P("fsdp"),
        P("fsdp"),
        P("fsdp"),
        P("fsdp", None),
        P("fsdp"),
        P("fsdp", None),
        P("fsdp"),
    )
    return jax.shard_map(
        shards,
        mesh=mesh,
        in_specs=placed,
        out_specs=(
            P(None, CTX, None, "fsdp", None),
            P(None, CTX, None, "fsdp", None),
            P("fsdp"),
            P("fsdp"),
            P("fsdp", None),
            P("fsdp"),
            P("fsdp"),
            P("fsdp", None),
            P("fsdp"),
            P("fsdp"),
            P("fsdp"),
            P("fsdp", None),
            P("fsdp"),
            P("fsdp", None),
            P("fsdp"),
        ),
        check_vma=False,
    )
```

profile of v0, /device:TPU:0, one launch (start us, length us, event | category | flops | bytes accessed | tf_op | source)
XLA Modules:
  0.0 879.7 jit_solution(5103445620654060094)
XLA Ops:
  9.0 41.7 %all_to_all.124 = bf16[4,128,3072]{2,1,0:T(8,128)(2,1)} all-to-all(bf16[4,128,3072]{2,1,0:T(8,128)(2,1)S(1)} %broadcast_in_dim.65), channel_id=1, replica_groups=mesh['zc'=4,'core'=2,'fsdp'=4] {'fsdp'}, dimensions={0} | all-to-all | bytes 6291456 | tf_op jit(solution)/shard_map/all_to_all | solution.py:108
  53.2 7.6 all-gather
  83.4 23.9 %all_to_all.125 = bf16[4,2,32,4,768]{4,2,1,0,3:T(8,128)(2,1)S(1)} all-to-all(bf16[4,2,32,4,768]{4,2,1,0,3:T(8,128)(2,1)S(1)} %pad_maximum_fusion), channel_id=1, replica_groups=mesh['zc'=4,'core'=2,'fsdp'=4] {'fsdp'}, dimensions={3} | all-to-all | bytes 3145728 | tf_op jit(solution)/shard_map/all_to_all | solution.py:230
  116.2 11.9 %all-to-all-done.3 = bf16[4,128,1024]{2,1,0:T(8,128)(2,1)} async-done(((bf16[4,128,1024]{2,1,0:T(8,128)(2,1)}), bf16[4,128,1024]{2,1,0:T(8,128)(2,1)}, u32[]{:S(2)}, u32[]{:S(2)}) %all-to-all-start.3) | async-done | bytes 1048608 | tf_op jit(solution)/shard_map/all_to_all | solution.py:108
  137.4 46.1 %all-to-all-done.4 = bf16[4,128,4096]{2,1,0:T(8,128)(2,1)} async-done(((bf16[4,128,4096]{2,1,0:T(8,128)(2,1)}), bf16[4,128,4096]{2,1,0:T(8,128)(2,1)}, u32[]{:S(2)}, u32[]{:S(2)}) %all-to-all-start.4) | async-done | bytes 4194336 | tf_op jit(solution)/shard_map/all_to_all | solution.py:108
  187.9 5.0 all-to-all-start.5
  193.5 46.2 %all-to-all-done.5 = bf16[4,512,1024]{2,1,0:T(8,128)(2,1)} async-done(((bf16[4,512,1024]{2,1,0:T(8,128)(2,1)}), bf16[4,512,1024]{2,1,0:T(8,128)(2,1)}, u32[]{:S(2)}, u32[]{:S(2)}) %all-to-all-start.5) | async-done | bytes 4194336 | tf_op jit(solution)/shard_map/all_to_all | solution.py:108
  241.6 6.5 fusion.98
  248.2 41.8 %while.26 = (s32[]{:T(128)}, bf16[4,256,256]{2,1,0:T(8,128)(2,1)S(1)}, f32[4,256,4]{1,2,0:T(4,128)}, s32[4,2048]{1,0:T(4,128)S(1)}, s32[4,256]{1,0:T(4,128)S(1)}...) while((s32[]{:T(128)}, ...), condition=%wide.region_11.12_spmd, body=%wide.region_2.11_spmd.sunk | while | flops 554240000 | bytes 35092604 | solution.py:246
  295.2 6.8 all-to-all-done.2
  306.8 9.5 %multiply_convert_fusion.4 = (bf16[256,4096]{1,0:T(8,128)(2,1)}, f32[256,4096]{1,0:T(8,128)}) fusion(f32[4096]{0:T(1024)S(1)} %bitcast.361, bf16[256,1024]{1,0:T(8,128)(2,1)S(1)} %add_convert_fusion.1, bf16[1024,4096]{1,0:T(8,128)(2,1)} %bitcast.375), kind=kOutput, calls=%fused_computation.142 | convolution fusion | flops 2157969408 | bytes 15220736 | tf_op jit(solution)/shard_map/dot_general | solution.py:256
  316.2 12.6 %convert_reduce_fusion = (f32[4096]{0:T(1024)}, bf16[256,4096]{1,0:T(8,128)(2,1)S(1)}) fusion(f32[256,4096]{1,0:T(8,128)} %get-tuple-element.305, bf16[4096,1024]{1,0:T(8,128)(2,1)} %bitcast.373, bf16[256,1024]{1,0:T(8,128)(2,1)S(1)} %bitcast.285), kind=kOutput, calls=%fused_computation.141 | convolution fusion | flops 2170548224 | bytes 15220736 | tf_op jit(solution)/shard_map/dot_general | solution.py:27
  341.2 7.2 convolution_convert_fusion.9
  349.3 118.0 %while.27 = (s32[]{:T(128)}, bf16[4,256,256]{2,1,0:T(8,128)(2,1)}, bf16[4,2048,256]{2,1,0:T(8,128)(2,1)}, bf16[4,2048,256]{2,1,0:T(8,128)(2,1)}, s32[4,2048]{1,0...) while((s32[]{:T(128)}, bf16[4,256,256]{2,1,0:T(8,128)(2,1)}, ...), condition=%wide.region_21.22_spmd, body=%wide.region_16.21_spmd.sunk | while | flops 1370029056 | bytes 166414960 | solution.py:280
  467.3 7.6 maximum_bitcast_fusion.5
  474.9 7.5 copy.115
  491.8 5.6 convolution_convert_fusion.8
  497.5 51.6 %all_to_all.127 = bf16[4,128,4096]{2,1,0:T(8,128)(2,1)} all-to-all(bf16[4,128,4096]{2,1,0:T(8,128)(2,1)} %bitcast.300), channel_id=1, replica_groups=mesh['zc'=4,'core'=2,'fsdp'=4] {'fsdp'}, dimensions={0} | all-to-all | bytes 8388608 | tf_op jit(solution)/shard_map/all_to_all | solution.py:131
  561.4 12.0 %reduce-scatter.10.cloned.1.call-done = bf16[1024,512]{1,0:T(8,128)(2,1)} async-done(((bf16[8192,512]{1,0:T(8,128)(2,1)}), bf16[1024,512]{1,0:T(8,128)(2,1)}) %reduce-scatter.10.cloned.1.call-update) | async-done | bytes 1048592 | tf_op jit(solution)/shard_map/reduce_scatter | solution.py:288
  581.1 5.2 all-to-all-done.8
  599.0 5.8 fusion.90
  612.5 49.4 %all_to_all.128 = bf16[4,512,1024]{2,1,0:T(8,128)(2,1)} all-to-all(bf16[4,512,1024]{2,1,0:T(8,128)(2,1)} %bitcast.301), channel_id=1, replica_groups=mesh['zc'=4,'core'=2,'fsdp'=4] {'fsdp'}, dimensions={0} | all-to-all | bytes 8388608 | tf_op jit(solution)/shard_map/all_to_all | solution.py:131
  667.2 13.4 %all_to_all.126 = bf16[4,128,1024]{2,1,0:T(8,128)(2,1)S(1)} all-to-all(bf16[4,128,1024]{2,1,0:T(8,128)(2,1)} %bitcast.329), channel_id=1, replica_groups=mesh['zc'=4,'core'=2,'fsdp'=4] {'fsdp'}, dimensions={0} | all-to-all | bytes 2097152 | tf_op jit(solution)/shard_map/all_to_all | solution.py:131
  685.4 12.1 %reduce-scatter.26.cloned.1.call-done = bf16[128,1024]{1,0:T(8,128)(2,1)} async-done(((bf16[512,1024]{1,0:T(8,128)(2,1)}), bf16[128,1024]{1,0:T(8,128)(2,1)}) %reduce-scatter.26.cloned.1.call-update) | async-done | bytes 262160 | tf_op jit(solution)/shard_map/reduce_scatter | solution.py:139
  698.5 16.4 %all-to-all-done.10 = bf16[4,128,3072]{2,1,0:T(8,128)(2,1)} async-done(((bf16[4,128,3072]{2,1,0:T(8,128)(2,1)}), bf16[4,128,3072]{2,1,0:T(8,128)(2,1)}, u32[]{:S(2)}, u32[]{:S(2)}) %all-to-all-start.10) | async-done | bytes 3145760 | tf_op jit(solution)/shard_map/all_to_all | solution.py:131
  718.6 7.0 all-gather.23.cloned.1.call-done
  725.6 28.7 %all-gather.27.cloned.1.call-done = bf16[512,1024]{1,0:T(8,128)(2,1)} async-done(((bf16[128,1024]{1,0:T(8,128)(2,1)}), bf16[512,1024]{1,0:T(8,128)(2,1)}) %all-gather.27.cloned.1.call-update) | async-done | bytes 1048592 | tf_op jit(solution)/shard_map/all_gather | solution.py:140
  756.0 7.2 fusion.78
  763.2 12.7 %reduce-scatter.18.cloned.1.call-done = bf16[32,1024]{1,0:T(8,128)(2,1)} async-done(((bf16[128,1024]{1,0:T(8,128)(2,1)}), bf16[32,1024]{1,0:T(8,128)(2,1)}) %reduce-scatter.18.cloned.1.call-update) | async-done | bytes 65552 | tf_op jit(solution)/shard_map/reduce_scatter | solution.py:139
  775.9 15.6 %all_gather.54 = bf16[128,1024]{1,0:T(8,128)(2,1)S(1)} all-gather(bf16[32,1024]{1,0:T(8,128)(2,1)} %reduce-scatter.18.cloned.1.call-done), channel_id=1, replica_groups=mesh['zc'=4,'core'=2,'fsdp'=4] {'zc'}, dimensions={0}, use_global_device_ids=true | all-gather | bytes 327680 | tf_op jit(solution)/shard_map/all_gather | solution.py:140
  800.7 18.2 %all_gather.52 = bf16[128,3072]{1,0:T(8,128)(2,1)} all-gather(bf16[32,3072]{1,0:T(8,128)(2,1)} %reduce-scatter.14.cloned.1.call-done), channel_id=1, replica_groups=mesh['zc'=4,'core'=2,'fsdp'=4] {'zc'}, dimensions={0}, use_global_device_ids=true | all-gather | bytes 983040 | tf_op jit(solution)/shard_map/all_gather | solution.py:140
  819.0 39.0 %psum.7 = f32[4,3072]{1,0:T(4,128)S(1)} all-reduce(f32[4,3072]{1,0:T(4,128)S(1)} %constant_dynamic-update-slice_fusion.7), channel_id=1, replica_groups=mesh['zc'=4,'core'=2,'fsdp'=4] {'zc','core','fsdp'}, use_global_device_ids=true, to_apply=%region_34.35 | all-reduce | flops 12288 | bytes 98304 | tf_op jit(solution)/shard_map/psum | solution.py:340
  (690 shorter events, 322.3 us)
Async XLA Ops:
  7.2 107.9 %copy-start = (bf16[256,4096]{1,0:T(8,128)(2,1)S(1)}, bf16[256,4096]{1,0:T(8,128)(2,1)}, u32[]{:S(2)}) copy-start(bf16[256,4096]{1,0:T(8,128)(2,1)} %param.32) | copy-start | bytes 6291460
  7.2 60.2 %all-gather.13.cloned.1.call-start = ((), (), s32[]{:S(2)}) async-start(), calls=%async_computation.23 | async-start | bytes 9437184 | tf_op jit(solution)/shard_map/all_gather | solution.py:115
  50.8 190.9 %all-gather.31.cloned.1.call-start = ((), (), s32[]{:S(2)}) async-start(), calls=%async_computation.41 | async-start | bytes 9437184 | tf_op jit(solution)/shard_map/all_gather | solution.py:239
  110.9 17.2 %all-to-all-start.3 = ((bf16[4,128,1024]{2,1,0:T(8,128)(2,1)}), bf16[4,128,1024]{2,1,0:T(8,128)(2,1)}, u32[]{:S(2)}, u32[]{:S(2)}) async-start(bf16[4,128,1024]{2,1,0:T(8,128)(2,1)} %broadcast_in_dim.66), calls=%async_computation.3 | async-start | bytes 2097152 | tf_op jit(solution)/shard_map/all_to_all | solution.py:108
  131.8 51.8 %all-to-all-start.4 = ((bf16[4,128,4096]{2,1,0:T(8,128)(2,1)}), bf16[4,128,4096]{2,1,0:T(8,128)(2,1)}, u32[]{:S(2)}, u32[]{:S(2)}) async-start(bf16[4,128,4096]{2,1,0:T(8,128)(2,1)} %broadcast_in_dim.67), calls=%async_computation.4 | async-start | bytes 8388608 | tf_op jit(solution)/shard_map/all_to_all | solution.py:108
  136.6 166.8 %all-gather.15.cloned.1.call-start = ((), (), s32[]{:S(2)}) async-start(), calls=%async_computation.24 | async-start | bytes 3145728 | tf_op jit(solution)/shard_map/all_gather | solution.py:115
  137.4 169.4 %all-gather.17.cloned.1.call-start = ((), (), s32[]{:S(2)}) async-start(), calls=%async_computation.25 | async-start | bytes 12582912 | tf_op jit(solution)/shard_map/all_gather | solution.py:115
  187.9 51.9 %all-to-all-start.5 = ((bf16[4,512,1024]{2,1,0:T(8,128)(2,1)}), bf16[4,512,1024]{2,1,0:T(8,128)(2,1)}, u32[]{:S(2)}, u32[]{:S(2)}) async-start(bf16[4,512,1024]{2,1,0:T(8,128)(2,1)} %broadcast_in_dim.68), calls=%async_computation.5 | async-start | bytes 8388608 | tf_op jit(solution)/shard_map/all_to_all | solution.py:108
  192.9 123.4 %all-gather.19.cloned.1.call-start = ((), (), s32[]{:S(2)}) async-start(), calls=%async_computation.26 | async-start | bytes 12582912 | tf_op jit(solution)/shard_map/all_gather | solution.py:115
  291.3 10.7 %all-to-all-start.2 = ((bf16[4,2,128,1,256]{4,1,0,3,2:T(2,128)(2,1)}), bf16[4,2,128,1,256]{4,1,0,3,2:T(2,128)(2,1)S(1)}, u32[]{:S(2)}, u32[]{:S(2)}) async-start(bf16[4,2,128,1,256]{4,1,0,3,2:T(2,128)(2,1)} %copy.104), calls=%async_computation.2 | async-start | bytes 1048576 | tf_op jit(solution)/shard_map/all_to_all | solution.py:249
  337.1 11.3 %all-to-all-start.6 = ((bf16[4,2,32,4,256]{4,2,1,0,3:T(8,128)(2,1)}), bf16[4,2,32,4,256]{4,2,1,0,3:T(8,128)(2,1)S(1)}, u32[]{:S(2)}, u32[]{:S(2)}) async-start(bf16[4,2,32,4,256]{4,2,1,0,3:T(8,128)(2,1)} %copy.107), calls=%async_computation.6 | async-start | bytes 1048576 | tf_op jit(solution)/shard_map/all_to_all | solution.py:277
  340.6 156.9 %reduce-scatter.20.cloned.1.call-start = ((), (), s32[]{:S(2)}) async-start(), calls=%async_computation.33 | async-start | bytes 12582912 | tf_op jit(solution)/shard_map/reduce_scatter | solution.py:129
  348.4 225.0 %reduce-scatter.10.cloned.1.call-start = ((), (), s32[]{:S(2)}) async-start(), calls=%async_computation.27 | async-start | bytes 9437184 | tf_op jit(solution)/shard_map/reduce_scatter | solution.py:288
  482.4 130.1 %reduce-scatter.24.cloned.1.call-start = ((), (), s32[]{:S(2)}) async-start(), calls=%async_computation.37 | async-start | bytes 12582912 | tf_op jit(solution)/shard_map/reduce_scatter | solution.py:129
  497.4 169.1 %reduce-scatter.22.cloned.1.call-start = ((), (), s32[]{:S(2)}) async-start(), calls=%async_computation.34 | async-start | bytes 1310720 | tf_op jit(solution)/shard_map/reduce_scatter | solution.py:139
  553.5 113.7 %reduce-scatter.16.cloned.1.call-start = ((), (), s32[]{:S(2)}) async-start(), calls=%async_computation.31 | async-start | bytes 3145728 | tf_op jit(solution)/shard_map/reduce_scatter | solution.py:129
  557.9 18.1 %all-to-all-start.7 = ((bf16[4,2,128,1,256]{4,1,0,3,2:T(2,128)(2,1)}), bf16[4,2,128,1,256]{4,1,0,3,2:T(2,128)(2,1)S(1)}, u32[]{:S(2)}, u32[]{:S(2)}) async-start(bf16[4,2,128,1,256]{4,1,0,3,2:T(2,128)(2,1)} %copy.110), calls=%async_computation.7 | async-start | bytes 1048576 | tf_op jit(solution)/shard_map/all_to_all | solution.py:299
  576.0 10.2 %all-to-all-start.8 = ((bf16[4,2,128,1,256]{4,1,0,3,2:T(2,128)(2,1)}), bf16[4,2,128,1,256]{4,1,0,3,2:T(2,128)(2,1)S(1)}, u32[]{:S(2)}, u32[]{:S(2)}) async-start(bf16[4,2,128,1,256]{4,1,0,3,2:T(2,128)(2,1)} %copy.116), calls=%async_computation.9 | async-start | bytes 1048576 | tf_op jit(solution)/shard_map/all_to_all | solution.py:302
  586.3 10.8 %all-to-all-start.9 = ((bf16[4,2,128,1,256]{4,1,0,3,2:T(2,128)(2,1)}), bf16[4,2,128,1,256]{4,1,0,3,2:T(2,128)(2,1)}, u32[]{:S(2)}, u32[]{:S(2)}) async-start(bf16[4,2,128,1,256]{4,1,0,3,2:T(2,128)(2,1)} %copy.119), calls=%async_computation.10 | async-start | bytes 1048576 | tf_op jit(solution)/shard_map/all_to_all | solution.py:305
  590.4 90.2 %reduce-scatter.12.cloned.1.call-start = ((), (), s32[]{:S(2)}) async-start(), calls=%async_computation.28 | async-start | bytes 9437184 | tf_op jit(solution)/shard_map/reduce_scatter | solution.py:129
  612.5 85.0 %reduce-scatter.26.cloned.1.call-start = ((), (), s32[]{:S(2)}) async-start(), calls=%async_computation.38 | async-start | bytes 1310720 | tf_op jit(solution)/shard_map/reduce_scatter | solution.py:139
  666.4 59.1 %all-gather.23.cloned.1.call-start = ((), (), s32[]{:S(2)}) async-start(), calls=%async_computation.35 | async-start | bytes 1310720 | tf_op jit(solution)/shard_map/all_gather | solution.py:140
  680.6 34.3 %all-to-all-start.10 = ((bf16[4,128,3072]{2,1,0:T(8,128)(2,1)}), bf16[4,128,3072]{2,1,0:T(8,128)(2,1)}, u32[]{:S(2)}, u32[]{:S(2)}) async-start(bf16[4,128,3072]{2,1,0:T(8,128)(2,1)} %bitcast.305), calls=%async_computation.12 | async-start | bytes 6291456 | tf_op jit(solution)/shard_map/all_to_all | solution.py:131
  685.3 69.1 %all-gather.27.cloned.1.call-start = ((), (), s32[]{:S(2)}) async-start(), calls=%async_computation.39 | async-start | bytes 1310720 | tf_op jit(solution)/shard_map/all_gather | solution.py:140
  697.5 78.4 %reduce-scatter.18.cloned.1.call-start = ((), (), s32[]{:S(2)}) async-start(), calls=%async_computation.32 | async-start | bytes 327680 | tf_op jit(solution)/shard_map/reduce_scatter | solution.py:139
  698.5 102.2 %reduce-scatter.14.cloned.1.call-start = ((), (), s32[]{:S(2)}) async-start(), calls=%async_computation.29 | async-start | bytes 983040 | tf_op jit(solution)/shard_map/reduce_scatter | solution.py:139
  718.5 142.4 %all-gather.25.cloned.1.call-start = ((), (), s32[]{:S(2)}) async-start(), calls=%async_computation.36 | async-start | bytes 3145728 | tf_op jit(solution)/shard_map/all_gather | solution.py:141
  725.6 139.4 %all-gather.29.cloned.1.call-start = ((), (), s32[]{:S(2)}) async-start(), calls=%async_computation.40 | async-start | bytes 3145728 | tf_op jit(solution)/shard_map/all_gather | solution.py:141
  754.4 114.8 %all-gather.21.cloned.1.call-start = ((), (), s32[]{:S(2)}) async-start(), calls=%async_computation.30 | async-start | bytes 2359296 | tf_op jit(solution)/shard_map/all_gather | solution.py:141
  797.3 62.2 %copy-start.18 = (f32[256,1024]{1,0:T(8,128)S(1)}, f32[256,1024]{1,0:T(8,128)}, u32[]{:S(2)}) copy-start(f32[256,1024]{1,0:T(8,128)} %copy-done.17) | copy-start | bytes 3145732
  797.3 62.2 %copy-start.21 = (bf16[4,1,2,32,1024]{4,3,2,1,0:T(8,128)(2,1)S(1)}, bf16[4,1,2,32,1024]{4,3,2,1,0:T(8,128)(2,1)}, u32[]{:S(2)}) copy-start(bf16[4,1,2,32,1024]{4,3,2,1,0:T(8,128)(2,1)} %param.21) | copy-start | bytes 1572868
  797.3 62.2 %copy-start.26 = (f32[256,1024]{1,0:T(8,128)S(1)}, f32[256,1024]{1,0:T(8,128)}, u32[]{:S(2)}) copy-start(f32[256,1024]{1,0:T(8,128)} %get-tuple-element.307) | copy-start | bytes 3145732
  (108 other events, 600.5 us)
Sparse Core Ops, SparseCore 0:
  50.9 16.4 all-gather.12
  109.8 81.4 all-gather.30
  192.9 9.0 all-gather.14
  203.4 21.0 all-gather.16
  239.9 19.8 all-gather.18
  348.5 17.7 reduce-scatter.19
  482.5 90.8 reduce-scatter.9
  575.7 14.8 reduce-scatter.23
  592.9 28.5 reduce-scatter.21
  624.2 8.2 reduce-scatter.15
  634.8 15.3 reduce-scatter.11
  666.5 30.8 reduce-scatter.25
  699.0 26.4 all-gather.22
  727.0 27.3 all-gather.26
  756.5 19.3 reduce-scatter.17
  778.6 22.0 reduce-scatter.13
  802.1 10.1 all-gather.24
  813.6 11.7 all-gather.28
  827.0 10.9 all-gather.20
where the time goes:
time: 889 us; the launch traced here: 880 us
  blocking collectives  263 us (30%)
  waiting for transfers between devices  216 us (24%)
  local copies, waits for them, and re-layouts  150 us (17%)
  matrix products  132 us (15%)
  other arithmetic  63.4 us (7%)
  starting transfers between devices  38.7 us (4%)
  between operations  15.6 us (2%)
    all_to_all x3, blocking collectives, reduce_weight_grad(): lax.all_to_all(grad.reshape((fsdp_size, -1) + grad.shape[1:]), 'fsdp', sp...  115 us
    all_to_all x3, waiting for transfers between devices, gather_weight(): lax.all_to_all(jnp.broadcast_to(piece[None], (fsdp_size,) + piece.shape),...  104 us
    dot_general x52, matrix products, contract_last(): lax.dot_general(left, right, (((1,), (1,)), ((), ())), preferred_element_...  52.5 us
    all_to_all x1, blocking collectives, gather_weight(): lax.all_to_all(jnp.broadcast_to(piece[None], (fsdp_size,) + piece.shape),...  41.7 us
    psum x1, blocking collectives, shards(): packed = lax.psum(packed.astype(jnp.float32), CTX + ('fsdp',))  39 us
    dot_general x36, matrix products, contract_first(): lax.dot_general(left, right, (((0,), (0,)), ((), ())), preferred_element_...  36 us
    all_gather x2, waiting for transfers between devices, reduce_weight_grad(): grad = lax.all_gather(grad, 'zc', axis=0, tiled=True)  35.7 us
    all_gather x2, blocking collectives, reduce_weight_grad(): grad = lax.all_gather(grad, 'zc', axis=0, tiled=True)  33.7 us
  transfers between devices with their start and end apart: 28, of which 14 were waited for; matrix products, arithmetic and copies ran while one was open for 31% of the time, Pallas kernels for 0%

commit v1 on v0

--- a/solution.py
+++ b/solution.py
@@ -337,7 +337,7 @@
         proj_bias_grad,
     )
     packed = jnp.concatenate([grad.reshape(fsdp_size, -1) for grad in vector_grads], axis=1)
-    packed = lax.psum(packed.astype(jnp.float32), CTX + ("fsdp",))
+    packed = jax.lax.all_gather(packed.astype(jnp.float32), axis_name=CTX + ("fsdp",)).sum(axis=0)
     packed = lax.dynamic_index_in_dim(packed, lax.axis_index("fsdp"), 0, keepdims=False)
     vector_totals = []
     offset = 0

time: 889 us -> 985 us (1.11)
  waiting for transfers between devices: 216 us -> 395 us
  blocking collectives: 263 us -> 164 us
  starting transfers between devices: 38.7 us -> 48.7 us
    all_to_all x1 -> x3, waiting for transfers between devices: 16.4 us -> 79.5 us  [reduce_weight_grad(): lax.all_to_all(grad.reshape((fsdp_size, -1) + grad.shape[1:]), 'fsdp', sp...]
    all_to_all x3 -> x1, blocking collectives: 115 us -> 53.5 us  [reduce_weight_grad(): lax.all_to_all(grad.reshape((fsdp_size, -1) + grad.shape[1:]), 'fsdp', sp...]
    reduce_scatter x1, waiting for transfers between devices: 12 us -> 61.3 us  [shards(): lax.psum_scatter(kv_grads.reshape(ctx_size * seq_count * pair_len, 2 * gr...]
    psum x1 -> x0, blocking collectives: 39 us -> none  [shards(): packed = lax.psum(packed.astype(jnp.float32), CTX + ('fsdp',))]
    all_gather x0 -> x1, waiting for transfers between devices: none -> 32.2 us  [shards(): jax.lax.all_gather(packed.astype(jnp.float32), axis_name=CTX + ('fsdp',))]
    all_gather x3, waiting for transfers between devices: 0.01 us -> 25.3 us  [reduce_weight_grad(): grad = lax.all_gather(grad, 'core', axis=0, tiled=True)]
    all_gather x2, waiting for transfers between devices: 35.7 us -> 21.5 us  [reduce_weight_grad(): grad = lax.all_gather(grad, 'zc', axis=0, tiled=True)]
    reduce_scatter x4, waiting for transfers between devices: 26.4 us -> 40.2 us  [reduce_weight_grad(): grad = lax.psum_scatter(grad, 'zc', scatter_dimension=0, tiled=True)]
  transfers between devices with their start and end apart: 28 -> 31, of which waited for: 14 -> 18; matrix products, arithmetic and copies ran while one was open for 31% -> 17% of each run, Pallas kernels for 0% -> 0%
where the time goes in v1:
time: 985 us; the launch traced here: 976 us
  waiting for transfers between devices  395 us (40%)
  blocking collectives  164 us (17%)
  local copies, waits for them, and re-layouts  154 us (16%)
  matrix products  131 us (13%)
  other arithmetic  65.2 us (7%)
  starting transfers between devices  48.7 us (5%)
  between operations  15.6 us (2%)
    all_to_all x3, waiting for transfers between devices, gather_weight(): lax.all_to_all(jnp.broadcast_to(piece[None], (fsdp_size,) + piece.shape),...  104 us
    all_to_all x3, waiting for transfers between devices, reduce_weight_grad(): lax.all_to_all(grad.reshape((fsdp_size, -1) + grad.shape[1:]), 'fsdp', sp...  79.5 us
    reduce_scatter x1, waiting for transfers between devices, shards(): lax.psum_scatter(kv_grads.reshape(ctx_size * seq_count * pair_len, 2 * gr...  61.3 us
    all_to_all x1, blocking collectives, reduce_weight_grad(): lax.all_to_all(grad.reshape((fsdp_size, -1) + grad.shape[1:]), 'fsdp', sp...  53.5 us
    dot_general x52, matrix products, contract_last(): lax.dot_general(left, right, (((1,), (1,)), ((), ())), preferred_element_...  51.9 us
    all_to_all x1, blocking collectives, gather_weight(): lax.all_to_all(jnp.broadcast_to(piece[None], (fsdp_size,) + piece.shape),...  41.7 us
    reduce_scatter x4, waiting for transfers between devices, reduce_weight_grad(): grad = lax.psum_scatter(grad, 'zc', scatter_dimension=0, tiled=True)  40.2 us
    dot_general x36, matrix products, contract_first(): lax.dot_general(left, right, (((0,), (0,)), ((), ())), preferred_element_...  35.9 us
  transfers between devices with their start and end apart: 31, of which 18 were waited for; matrix products, arithmetic and copies ran while one was open for 17% of the time, Pallas kernels for 0%

profile of v1, /device:TPU:0, one launch (start us, length us, event | category | flops | bytes accessed | tf_op | source)
XLA Modules:
  0.0 975.7 jit_solution(10298605169202098431)
XLA Ops:
  9.0 41.7 %all_to_all.124 = bf16[4,128,3072]{2,1,0:T(8,128)(2,1)} all-to-all(bf16[4,128,3072]{2,1,0:T(8,128)(2,1)S(1)} %broadcast_in_dim.65), channel_id=1, replica_groups=mesh['zc'=4,'core'=2,'fsdp'=4] {'fsdp'}, dimensions={0} | all-to-all | bytes 6291456 | tf_op jit(solution)/shard_map/all_to_all | solution.py:108
  53.2 7.6 all-gather
  83.4 23.9 %all_to_all.125 = bf16[4,2,32,4,768]{4,2,1,0,3:T(8,128)(2,1)S(1)} all-to-all(bf16[4,2,32,4,768]{4,2,1,0,3:T(8,128)(2,1)S(1)} %pad_maximum_fusion), channel_id=1, replica_groups=mesh['zc'=4,'core'=2,'fsdp'=4] {'fsdp'}, dimensions={3} | all-to-all | bytes 3145728 | tf_op jit(solution)/shard_map/all_to_all | solution.py:230
  116.2 11.9 %all-to-all-done.3 = bf16[4,128,1024]{2,1,0:T(8,128)(2,1)} async-done(((bf16[4,128,1024]{2,1,0:T(8,128)(2,1)}), bf16[4,128,1024]{2,1,0:T(8,128)(2,1)}, u32[]{:S(2)}, u32[]{:S(2)}) %all-to-all-start.3) | async-done | bytes 1048608 | tf_op jit(solution)/shard_map/all_to_all | solution.py:108
  137.4 46.1 %all-to-all-done.4 = bf16[4,128,4096]{2,1,0:T(8,128)(2,1)} async-done(((bf16[4,128,4096]{2,1,0:T(8,128)(2,1)}), bf16[4,128,4096]{2,1,0:T(8,128)(2,1)}, u32[]{:S(2)}, u32[]{:S(2)}) %all-to-all-start.4) | async-done | bytes 4194336 | tf_op jit(solution)/shard_map/all_to_all | solution.py:108
  193.7 46.1 %all-to-all-done.5 = bf16[4,512,1024]{2,1,0:T(8,128)(2,1)} async-done(((bf16[4,512,1024]{2,1,0:T(8,128)(2,1)}), bf16[4,512,1024]{2,1,0:T(8,128)(2,1)}, u32[]{:S(2)}, u32[]{:S(2)}) %all-to-all-start.5) | async-done | bytes 4194336 | tf_op jit(solution)/shard_map/all_to_all | solution.py:108
  241.7 6.5 fusion.98
  248.2 41.8 %while.26 = (s32[]{:T(128)}, bf16[4,256,256]{2,1,0:T(8,128)(2,1)S(1)}, f32[4,256,4]{1,2,0:T(4,128)}, s32[4,2048]{1,0:T(4,128)S(1)}, s32[4,256]{1,0:T(4,128)S(1)}...) while((s32[]{:T(128)}, ...), condition=%wide.region_11.12_spmd, body=%wide.region_2.11_spmd.sunk | while | flops 554240000 | bytes 35092604 | solution.py:246
  295.5 6.8 all-to-all-done.2
  306.7 9.5 multiply_convert_fusion.4
  316.3 12.1 %convert_reduce_fusion = (f32[4096]{0:T(1024)}, bf16[256,4096]{1,0:T(8,128)(2,1)S(1)}) fusion(f32[256,4096]{1,0:T(8,128)} %get-tuple-element.305, bf16[4096,1024]{1,0:T(8,128)(2,1)} %bitcast.375, bf16[256,1024]{1,0:T(8,128)(2,1)S(1)} %bitcast.286), kind=kOutput, calls=%fused_computation.141 | convolution fusion | flops 2170548224 | bytes 15220736 | tf_op jit(solution)/shard_map/dot_general | solution.py:27
  340.4 6.3 all-to-all-done.6
  347.5 117.9 %while.27 = (s32[]{:T(128)}, bf16[4,256,256]{2,1,0:T(8,128)(2,1)}, bf16[4,2048,256]{2,1,0:T(8,128)(2,1)}, bf16[4,2048,256]{2,1,0:T(8,128)(2,1)}, s32[4,2048]{1,0...) while((s32[]{:T(128)}, bf16[4,256,256]{2,1,0:T(8,128)(2,1)}, ...), condition=%wide.region_21.22_spmd, body=%wide.region_16.21_spmd.sunk | while | flops 1370029056 | bytes 166414960 | solution.py:280
  465.4 7.5 maximum_bitcast_fusion.5
  473.0 7.6 copy.115
  482.5 5.9 convolution_convert_fusion.9
  509.0 61.3 %reduce-scatter.10.cloned.1.call-done = bf16[1024,512]{1,0:T(8,128)(2,1)} async-done(((bf16[8192,512]{1,0:T(8,128)(2,1)}), bf16[1024,512]{1,0:T(8,128)(2,1)}) %reduce-scatter.10.cloned.1.call-update) | async-done | bytes 1048592 | tf_op jit(solution)/shard_map/reduce_scatter | solution.py:288
  576.5 10.9 %reduce-scatter.20.cloned.1.call-done = bf16[512,4096]{1,0:T(8,128)(2,1)} async-done(((bf16[1024,4096]{1,0:T(8,128)(2,1)}), bf16[512,4096]{1,0:T(8,128)(2,1)}) %reduce-scatter.20.cloned.1.call-update) | async-done | bytes 4194320 | tf_op jit(solution)/shard_map/reduce_scatter | solution.py:129
  593.6 46.8 %all-to-all-done.12 = bf16[4,128,4096]{2,1,0:T(8,128)(2,1)} async-done(((bf16[4,128,4096]{2,1,0:T(8,128)(2,1)}), bf16[4,128,4096]{2,1,0:T(8,128)(2,1)}, u32[]{:S(2)}, u32[]{:S(2)}) %all-to-all-start.12) | async-done | bytes 4194336 | tf_op jit(solution)/shard_map/all_to_all | solution.py:131
  668.1 53.5 %all_to_all.126 = bf16[4,512,1024]{2,1,0:T(8,128)(2,1)} all-to-all(bf16[4,512,1024]{2,1,0:T(8,128)(2,1)} %bitcast.301), channel_id=1, replica_groups=mesh['zc'=4,'core'=2,'fsdp'=4] {'fsdp'}, dimensions={0} | all-to-all | bytes 8388608 | tf_op jit(solution)/shard_map/all_to_all | solution.py:131
  738.0 15.0 %reduce-scatter.26.cloned.1.call-done = bf16[128,1024]{1,0:T(8,128)(2,1)} async-done(((bf16[512,1024]{1,0:T(8,128)(2,1)}), bf16[128,1024]{1,0:T(8,128)(2,1)}) %reduce-scatter.26.cloned.1.call-update) | async-done | bytes 262160 | tf_op jit(solution)/shard_map/reduce_scatter | solution.py:139
  753.0 19.8 %all-to-all-done.10 = bf16[4,128,3072]{2,1,0:T(8,128)(2,1)} async-done(((bf16[4,128,3072]{2,1,0:T(8,128)(2,1)}), bf16[4,128,3072]{2,1,0:T(8,128)(2,1)}, u32[]{:S(2)}, u32[]{:S(2)}) %all-to-all-start.10) | async-done | bytes 3145760 | tf_op jit(solution)/shard_map/all_to_all | solution.py:131
  781.1 12.9 %all-to-all-done.11 = bf16[4,128,1024]{2,1,0:T(8,128)(2,1)} async-done(((bf16[4,128,1024]{2,1,0:T(8,128)(2,1)}), bf16[4,128,1024]{2,1,0:T(8,128)(2,1)}, u32[]{:S(2)}, u32[]{:S(2)}) %all-to-all-start.11) | async-done | bytes 1048608 | tf_op jit(solution)/shard_map/all_to_all | solution.py:131
  802.1 21.5 %all-gather.30.cloned.1.call-done = bf16[512,1024]{1,0:T(8,128)(2,1)} async-done(((bf16[128,1024]{1,0:T(8,128)(2,1)}), bf16[512,1024]{1,0:T(8,128)(2,1)}) %all-gather.30.cloned.1.call-update) | async-done | bytes 1048592 | tf_op jit(solution)/shard_map/all_gather | solution.py:140
  823.7 25.2 %reduce-scatter.14.cloned.1.call-done = bf16[32,3072]{1,0:T(8,128)(2,1)} async-done(((bf16[128,3072]{1,0:T(8,128)(2,1)}), bf16[32,3072]{1,0:T(8,128)(2,1)}) %reduce-scatter.14.cloned.1.call-update) | async-done | bytes 196624 | tf_op jit(solution)/shard_map/reduce_scatter | solution.py:139
  848.9 20.7 %all_gather.60 = bf16[128,3072]{1,0:T(8,128)(2,1)} all-gather(bf16[32,3072]{1,0:T(8,128)(2,1)} %reduce-scatter.14.cloned.1.call-done), channel_id=1, replica_groups=mesh['zc'=4,'core'=2,'fsdp'=4] {'zc'}, dimensions={0}, use_global_device_ids=true | all-gather | bytes 983040 | tf_op jit(solution)/shard_map/all_gather | solution.py:140
  869.6 7.2 fusion.78
  876.8 14.8 %all_gather.62 = bf16[128,1024]{1,0:T(8,128)(2,1)S(1)} all-gather(bf16[32,1024]{1,0:T(8,128)(2,1)} %reduce-scatter.18.cloned.1.call-done), channel_id=1, replica_groups=mesh['zc'=4,'core'=2,'fsdp'=4] {'zc'}, dimensions={0}, use_global_device_ids=true | all-gather | bytes 327680 | tf_op jit(solution)/shard_map/all_gather | solution.py:140
  896.4 32.2 %all-gather.36.cloned.1.call-done = f32[32,4,3072]{2,1,0:T(4,128)} async-done(((f32[1,4,3072]{2,1,0:T(4,128)}), f32[32,4,3072]{2,1,0:T(4,128)}) %all-gather.36.cloned.1.call-update) | async-done | bytes 1572880 | tf_op jit(solution)/shard_map/all_gather | solution.py:340
  931.6 7.9 all-gather.28.cloned.1.call-done
  943.6 9.2 all-gather.32.cloned.1.call-done
  957.1 8.2 all-gather.24.cloned.1.call-done
  (695 shorter events, 351.9 us)
Async XLA Ops:
  7.2 107.9 %copy-start = (bf16[256,4096]{1,0:T(8,128)(2,1)S(1)}, bf16[256,4096]{1,0:T(8,128)(2,1)}, u32[]{:S(2)}) copy-start(bf16[256,4096]{1,0:T(8,128)(2,1)} %param.32) | copy-start | bytes 6291460
  7.2 60.2 %all-gather.16.cloned.1.call-start = ((), (), s32[]{:S(2)}) async-start(), calls=%async_computation.23 | async-start | bytes 9437184 | tf_op jit(solution)/shard_map/all_gather | solution.py:115
  50.8 190.9 %all-gather.34.cloned.1.call-start = ((), (), s32[]{:S(2)}) async-start(), calls=%async_computation.41 | async-start | bytes 9437184 | tf_op jit(solution)/shard_map/all_gather | solution.py:239
  110.9 17.2 %all-to-all-start.3 = ((bf16[4,128,1024]{2,1,0:T(8,128)(2,1)}), bf16[4,128,1024]{2,1,0:T(8,128)(2,1)}, u32[]{:S(2)}, u32[]{:S(2)}) async-start(bf16[4,128,1024]{2,1,0:T(8,128)(2,1)} %broadcast_in_dim.66), calls=%async_computation.3 | async-start | bytes 2097152 | tf_op jit(solution)/shard_map/all_to_all | solution.py:108
  131.8 51.8 %all-to-all-start.4 = ((bf16[4,128,4096]{2,1,0:T(8,128)(2,1)}), bf16[4,128,4096]{2,1,0:T(8,128)(2,1)}, u32[]{:S(2)}, u32[]{:S(2)}) async-start(bf16[4,128,4096]{2,1,0:T(8,128)(2,1)} %broadcast_in_dim.67), calls=%async_computation.4 | async-start | bytes 8388608 | tf_op jit(solution)/shard_map/all_to_all | solution.py:108
  136.7 167.1 %all-gather.18.cloned.1.call-start = ((), (), s32[]{:S(2)}) async-start(), calls=%async_computation.24 | async-start | bytes 3145728 | tf_op jit(solution)/shard_map/all_gather | solution.py:115
  137.4 169.3 %all-gather.20.cloned.1.call-start = ((), (), s32[]{:S(2)}) async-start(), calls=%async_computation.25 | async-start | bytes 12582912 | tf_op jit(solution)/shard_map/all_gather | solution.py:115
  187.9 51.9 %all-to-all-start.5 = ((bf16[4,512,1024]{2,1,0:T(8,128)(2,1)}), bf16[4,512,1024]{2,1,0:T(8,128)(2,1)}, u32[]{:S(2)}, u32[]{:S(2)}) async-start(bf16[4,512,1024]{2,1,0:T(8,128)(2,1)} %broadcast_in_dim.68), calls=%async_computation.5 | async-start | bytes 8388608 | tf_op jit(solution)/shard_map/all_to_all | solution.py:108
  192.9 123.4 %all-gather.22.cloned.1.call-start = ((), (), s32[]{:S(2)}) async-start(), calls=%async_computation.26 | async-start | bytes 12582912 | tf_op jit(solution)/shard_map/all_gather | solution.py:115
  291.4 10.9 %all-to-all-start.2 = ((bf16[4,2,128,1,256]{4,1,0,3,2:T(2,128)(2,1)}), bf16[4,2,128,1,256]{4,1,0,3,2:T(2,128)(2,1)S(1)}, u32[]{:S(2)}, u32[]{:S(2)}) async-start(bf16[4,2,128,1,256]{4,1,0,3,2:T(2,128)(2,1)} %copy.104), calls=%async_computation.2 | async-start | bytes 1048576 | tf_op jit(solution)/shard_map/all_to_all | solution.py:249
  336.6 10.0 %all-to-all-start.6 = ((bf16[4,2,32,4,256]{4,2,1,0,3:T(8,128)(2,1)}), bf16[4,2,32,4,256]{4,2,1,0,3:T(8,128)(2,1)S(1)}, u32[]{:S(2)}, u32[]{:S(2)}) async-start(bf16[4,2,32,4,256]{4,2,1,0,3:T(8,128)(2,1)} %copy.107), calls=%async_computation.6 | async-start | bytes 1048576 | tf_op jit(solution)/shard_map/all_to_all | solution.py:277
  340.1 230.1 %reduce-scatter.10.cloned.1.call-start = ((), (), s32[]{:S(2)}) async-start(), calls=%async_computation.27 | async-start | bytes 9437184 | tf_op jit(solution)/shard_map/reduce_scatter | solution.py:288
  480.6 106.8 %reduce-scatter.20.cloned.1.call-start = ((), (), s32[]{:S(2)}) async-start(), calls=%async_computation.33 | async-start | bytes 12582912 | tf_op jit(solution)/shard_map/reduce_scatter | solution.py:129
  488.4 179.7 %reduce-scatter.24.cloned.1.call-start = ((), (), s32[]{:S(2)}) async-start(), calls=%async_computation.37 | async-start | bytes 12582912 | tf_op jit(solution)/shard_map/reduce_scatter | solution.py:129
  505.5 67.3 %all-to-all-start.7 = ((bf16[4,2,128,1,256]{4,1,0,3,2:T(2,128)(2,1)}), bf16[4,2,128,1,256]{4,1,0,3,2:T(2,128)(2,1)S(1)}, u32[]{:S(2)}, u32[]{:S(2)}) async-start(bf16[4,2,128,1,256]{4,1,0,3,2:T(2,128)(2,1)} %copy.110), calls=%async_computation.7 | async-start | bytes 1048576 | tf_op jit(solution)/shard_map/all_to_all | solution.py:299
  572.8 14.5 %all-to-all-start.8 = ((bf16[4,2,128,1,256]{4,1,0,3,2:T(2,128)(2,1)}), bf16[4,2,128,1,256]{4,1,0,3,2:T(2,128)(2,1)S(1)}, u32[]{:S(2)}, u32[]{:S(2)}) async-start(bf16[4,2,128,1,256]{4,1,0,3,2:T(2,128)(2,1)} %copy.116), calls=%async_computation.9 | async-start | bytes 1048576 | tf_op jit(solution)/shard_map/all_to_all | solution.py:302
  587.4 53.1 %all-to-all-start.12 = ((bf16[4,128,4096]{2,1,0:T(8,128)(2,1)}), bf16[4,128,4096]{2,1,0:T(8,128)(2,1)}, u32[]{:S(2)}, u32[]{:S(2)}) async-start(bf16[4,128,4096]{2,1,0:T(8,128)(2,1)} %bitcast.302), calls=%async_computation.18 | async-start | bytes 8388608 | tf_op jit(solution)/shard_map/all_to_all | solution.py:131
  640.4 12.4 %all-to-all-start.9 = ((bf16[4,2,128,1,256]{4,1,0,3,2:T(2,128)(2,1)}), bf16[4,2,128,1,256]{4,1,0,3,2:T(2,128)(2,1)}, u32[]{:S(2)}, u32[]{:S(2)}) async-start(bf16[4,2,128,1,256]{4,1,0,3,2:T(2,128)(2,1)} %copy.119), calls=%async_computation.10 | async-start | bytes 1048576 | tf_op jit(solution)/shard_map/all_to_all | solution.py:305
  644.6 87.9 %reduce-scatter.22.cloned.1.call-start = ((), (), s32[]{:S(2)}) async-start(), calls=%async_computation.34 | async-start | bytes 1310720 | tf_op jit(solution)/shard_map/reduce_scatter | solution.py:139
  651.0 82.2 %reduce-scatter.12.cloned.1.call-start = ((), (), s32[]{:S(2)}) async-start(), calls=%async_computation.28 | async-start | bytes 9437184 | tf_op jit(solution)/shard_map/reduce_scatter | solution.py:129
  668.0 84.9 %reduce-scatter.26.cloned.1.call-start = ((), (), s32[]{:S(2)}) async-start(), calls=%async_computation.38 | async-start | bytes 1310720 | tf_op jit(solution)/shard_map/reduce_scatter | solution.py:139
  726.0 50.5 %reduce-scatter.16.cloned.1.call-start = ((), (), s32[]{:S(2)}) async-start(), calls=%async_computation.31 | async-start | bytes 3145728 | tf_op jit(solution)/shard_map/reduce_scatter | solution.py:129
  732.5 68.9 %all-gather.26.cloned.1.call-start = ((), (), s32[]{:S(2)}) async-start(), calls=%async_computation.35 | async-start | bytes 1310720 | tf_op jit(solution)/shard_map/all_gather | solution.py:140
  733.2 39.6 %all-to-all-start.10 = ((bf16[4,128,3072]{2,1,0:T(8,128)(2,1)}), bf16[4,128,3072]{2,1,0:T(8,128)(2,1)}, u32[]{:S(2)}, u32[]{:S(2)}) async-start(bf16[4,128,3072]{2,1,0:T(8,128)(2,1)} %bitcast.306), calls=%async_computation.12 | async-start | bytes 6291456 | tf_op jit(solution)/shard_map/all_to_all | solution.py:131
  737.9 85.7 %all-gather.30.cloned.1.call-start = ((), (), s32[]{:S(2)}) async-start(), calls=%async_computation.39 | async-start | bytes 1310720 | tf_op jit(solution)/shard_map/all_gather | solution.py:140
  753.0 95.9 %reduce-scatter.14.cloned.1.call-start = ((), (), s32[]{:S(2)}) async-start(), calls=%async_computation.29 | async-start | bytes 983040 | tf_op jit(solution)/shard_map/reduce_scatter | solution.py:139
  776.5 17.4 %all-to-all-start.11 = ((bf16[4,128,1024]{2,1,0:T(8,128)(2,1)}), bf16[4,128,1024]{2,1,0:T(8,128)(2,1)}, u32[]{:S(2)}, u32[]{:S(2)}) async-start(bf16[4,128,1024]{2,1,0:T(8,128)(2,1)} %bitcast.330), calls=%async_computation.15 | async-start | bytes 2097152 | tf_op jit(solution)/shard_map/all_to_all | solution.py:131
  780.8 96.0 %reduce-scatter.18.cloned.1.call-start = ((), (), s32[]{:S(2)}) async-start(), calls=%async_computation.32 | async-start | bytes 327680 | tf_op jit(solution)/shard_map/reduce_scatter | solution.py:139
  796.2 132.4 %all-gather.36.cloned.1.call-start = ((), (), s32[]{:S(2)}) async-start(), calls=%async_computation.42 | async-start | bytes 1622016 | tf_op jit(solution)/shard_map/all_gather | solution.py:340
  801.3 138.2 %all-gather.28.cloned.1.call-start = ((), (), s32[]{:S(2)}) async-start(), calls=%async_computation.36 | async-start | bytes 3145728 | tf_op jit(solution)/shard_map/all_gather | solution.py:141
  801.9 150.9 %all-gather.32.cloned.1.call-start = ((), (), s32[]{:S(2)}) async-start(), calls=%async_computation.40 | async-start | bytes 3145728 | tf_op jit(solution)/shard_map/all_gather | solution.py:141
  823.6 141.6 %all-gather.24.cloned.1.call-start = ((), (), s32[]{:S(2)}) async-start(), calls=%async_computation.30 | async-start | bytes 2359296 | tf_op jit(solution)/shard_map/all_gather | solution.py:141
  (111 other events, 695.5 us)
Sparse Core Ops, SparseCore 0:
  50.9 16.4 all-gather.15
  109.8 81.4 all-gather.33
  192.9 9.0 all-gather.17
  203.4 21.0 all-gather.19
  239.9 19.8 all-gather.21
  480.7 89.5 reduce-scatter.9
  572.5 14.8 reduce-scatter.19
  589.7 17.6 reduce-scatter.23
  651.2 28.8 reduce-scatter.21
  682.2 12.5 reduce-scatter.11
  726.2 26.7 reduce-scatter.25
  755.6 8.2 reduce-scatter.15
  765.5 29.2 all-gather.25
  796.2 27.3 all-gather.29
  826.3 22.5 reduce-scatter.13
  851.0 20.8 reduce-scatter.17
  875.3 53.2 all-gather.35
  930.0 9.4 all-gather.27
  941.0 11.7 all-gather.31
  954.2 10.9 all-gather.23
